TPU v7x, 256 devices: a whole 4x4x8 slice. The times are simulated.
256 devices in a mesh: docs: 32 (over y, x, z_hi), dims: 8 (over z_lo, core).
Axes of the slice: x: 4, y: 4, z: 8 (z_hi: 2, z_lo: 4; z = z_hi * 4 + z_lo), core: 2. Of those that a mesh axis runs over, the one named last changes fastest.
Arguments:
- queries: bfloat16 [16384, 3072], P('docs', 'dims'), may hold values from -6 to 6
- doc_vectors: bfloat16 [65536, 3072], P('docs', 'dims'), may hold values from -6 to 6
- surv_pairs: int32 [32, 144], P('docs'), may hold values from 0 to 2047
- surv_count: int32 [32], P('docs'), may hold values from 36 to 144, as said below
- short_pairs: int32 [32, 96], P('docs'), may hold values from 0 to 2047
- short_count: int32 [32], P('docs'), may hold values from 24 to 96, as said below
Outputs:
- prefix_scores: float32 [32, 144, 128, 128], P('docs', None, 'dims')
- full_scores: float32 [32, 96, 128, 128], P('docs', None, 'dims')
Inputs may be any that keep to these rules, and one draw needn't show every extreme that they name: `surv_count`: each shard's live survivor slots; some shard has all 144 slots live. `short_count`: each shard's live shortlist slots; some shard has all 96 slots live.
All inputs are finite; a program needn't handle non-finite values.
Results may differ from a plain program's by a relative error of at most 0.0003.
Values may be sent and summed in bfloat16 or wider, within the bound.
No kernel may reach another device: no remote copies, remote signals or barrier semaphores. Data moves between devices by JAX's collectives and lax.ppermute only.
A program may use at most 128 MiB of HBM per device.

v0:
```python
import jax
import jax.numpy as jnp
from jax import lax
from jax.sharding import PartitionSpec as P

D = 3072
PREFIX = 768
QB = 128
DB = 128


def shards(queries, doc_vectors, surv_pairs, surv_count, short_pairs, short_count):
    every_query = lax.all_gather(queries, "docs", axis=0, tiled=True)
    slice_width = queries.shape[1]
    query_blocks = every_query.reshape(-1, QB, slice_width)
    doc_blocks = doc_vectors.reshape(-1, DB, slice_width)
    local_blocks = doc_blocks.shape[0]
    columns = lax.axis_index("dims") * slice_width + jnp.arange(slice_width)
    prefix_blocks = jnp.where(
        columns[None, None, :] < PREFIX, doc_blocks, jnp.zeros((), doc_blocks.dtype)
    )

    def pair_products(pair_ids, doc_side):
        picked_queries = jnp.take(query_blocks, pair_ids // local_blocks, axis=0)
        picked_docs = jnp.take(doc_side, pair_ids % local_blocks, axis=0)
        return jnp.einsum(
            "gqc,gdc->gqd", picked_queries, picked_docs, preferred_element_type=jnp.float32
        )

    def score_slots(pair_list, doc_side):
        return pair_products(pair_list, doc_side)

    full_terms = score_slots(short_pairs[0], doc_blocks)
    prefix_terms = score_slots(surv_pairs[0], prefix_blocks)
    prefix_sum, full_sum = (
        lax.psum_scatter(prefix_terms, "dims", scatter_dimension=1, tiled=True),
        lax.psum_scatter(full_terms, "dims", scatter_dimension=1, tiled=True),
    )

    def finish(summed, live_count, factor):
        slots = jnp.arange(summed.shape[0])
        return jnp.where(slots[:, None, None] < live_count, summed * factor, jnp.float32(0.0))

    prefix_out = finish(prefix_sum, surv_count[0], float(PREFIX) ** (-0.5))
    full_out = finish(full_sum, short_count[0], float(D) ** (-0.5))
    return (prefix_out[None], full_out[None])


def solution(mesh):
    placed = (
        P("docs", "dims"),
        P("docs", "dims"),
        P("docs", None),
        P("docs"),
        P("docs", None),
        P("docs"),
    )
    return jax.shard_map(
        shards,
        mesh=mesh,
        in_specs=placed,
        out_specs=(P("docs", None, "dims", None), P("docs", None, "dims", None)),
        check_vma=False,
    )
```

profile of v0, /device:TPU:2, one launch (start us, length us, event | category | flops | bytes accessed | tf_op | source)
XLA Modules:
  0.0 420.8 jit_solution(5105553798239716115)
XLA Ops:
  7.2 0.0 all-gather.2.cloned.1.call-start
  7.2 0.7 all-gather.2.cloned.1.call-update
  7.9 0.0 reduce-scatter.5.cloned.1.call-start
  7.9 0.7 fusion.12
  8.6 0.0 copy-start.2
  8.6 9.3 %gather_fusion.3 = bf16[96,128,384]{2,1,0:T(8,128)(2,1)} fusion(bf16[16,128,384]{2,1,0:T(8,128)(2,1)} %bitcast.65, s32[1024]{0:T(1024)S(1)} %get-tuple-element.10), kind=kCustom, calls=%fused_computation.3 | custom fusion | bytes 18874752 | tf_op jit(solution)/shard_map/jit(_take)/gather | solution.py:25
  18.0 0.0 copy-done.2
  18.0 195.2 %all-gather.2.cloned.1.call-done = bf16[16384,384]{1,0:T(8,128)(2,1)} async-done(((bf16[512,384]{1,0:T(8,128)(2,1)}), bf16[16384,384]{1,0:T(8,128)(2,1)}) %all-gather.2.cloned.1.call-update) | async-done | bytes 12582928 | tf_op jit(solution)/shard_map/all_gather | solution.py:13
  213.2 12.5 %gather_fusion.2 = bf16[96,128,384]{2,1,0:T(8,128)(2,1)} fusion(bf16[128,128,384]{2,1,0:T(8,128)(2,1)} %bitcast.67, s32[1024]{0:T(1024)S(1)} %get-tuple-element.11), kind=kCustom, calls=%fused_computation.2 | custom fusion | bytes 18874752 | tf_op jit(solution)/shard_map/jit(_take)/gather | solution.py:24
  225.7 0.0 copy-start.1
  225.7 0.0 copy-start
  225.7 10.4 %fusion.5 = f32[96,128,128]{2,1,0:T(8,128)} fusion(bf16[96,128,384]{2,1,0:T(8,128)(2,1)} %gather_fusion.3, bf16[96,128,384]{2,1,0:T(8,128)(2,1)} %gather_fusion.2, pred[96]{0:T(512)(128)(4,1)S(1)} %get-tuple-element.7, pred[96]{0:T(512)(128)(4,1)S(1)} %get-tuple-element.6), kind=kOutput, calls=%fused_computation.9 | convolution fusion | flops 1217396736 | bytes 25166016 | tf_op jit(solution)/shard_map/gqc,gdc->gqd/dot_general | solution.py:26
  236.1 0.0 reduce-scatter.5.cloned.1.call-update
  236.1 0.2 reduce-scatter.3.cloned.1.call-start
  236.4 0.0 copy-done.1
  236.4 0.0 copy-done
  236.4 0.2 broadcast_select_fusion
  236.6 9.5 %gather_fusion.1 = bf16[144,128,384]{2,1,0:T(8,128)(2,1)} fusion(bf16[16,128,384]{2,1,0:T(8,128)(2,1)S(1)} %broadcast_select_fusion, s32[1024]{0:T(1024)S(1)} %pad_clamp_fusion.2), kind=kCustom, calls=%fused_computation.1 | custom fusion | bytes 28312128 | tf_op jit(solution)/shard_map/jit(_take)/gather | solution.py:25
  246.1 14.2 %gather_fusion = bf16[144,128,384]{2,1,0:T(8,128)(2,1)} fusion(bf16[128,128,384]{2,1,0:T(8,128)(2,1)} %bitcast.68, s32[1024]{0:T(1024)S(1)} %pad_clamp_fusion.3), kind=kCustom, calls=%fused_computation | custom fusion | bytes 28312128 | tf_op jit(solution)/shard_map/jit(_take)/gather | solution.py:24
  260.3 14.9 %fusion = f32[144,128,128]{2,1,0:T(8,128)} fusion(bf16[144,128,384]{2,1,0:T(8,128)(2,1)} %gather_fusion.1, bf16[144,128,384]{2,1,0:T(8,128)(2,1)} %gather_fusion, pred[144]{0:T(512)(128)(4,1)S(1)} %get-tuple-element.5, pred[144]{0:T(512)(128)(4,1)S(1)} %get-tuple-element.4), kind=kOutput, calls=%fused_computation.4 | convolution fusion | flops 1826095104 | bytes 37749024 | tf_op jit(solution)/shard_map/gqc,gdc->gqd/dot_general | solution.py:26
  275.2 0.0 reduce-scatter.3.cloned.1.call-update
  276.5 29.3 %reduce-scatter.5.cloned.1.call-done = f32[96,16,128]{2,1,0:T(8,128)} async-done(((f32[96,128,128]{2,1,0:T(8,128)}), f32[96,16,128]{2,1,0:T(8,128)}) %reduce-scatter.5.cloned.1.call-update) | async-done | bytes 786448 | tf_op jit(solution)/shard_map/reduce_scatter | solution.py:37
  305.9 2.2 select_bitcast_fusion.1
  308.0 103.7 %reduce-scatter.3.cloned.1.call-done = f32[144,16,128]{2,1,0:T(8,128)} async-done(((f32[144,128,128]{2,1,0:T(8,128)}), f32[144,16,128]{2,1,0:T(8,128)}) %reduce-scatter.3.cloned.1.call-update) | async-done | bytes 1179664 | tf_op jit(solution)/shard_map/reduce_scatter | solution.py:36
  411.8 2.5 select_bitcast_fusion
  (10 shorter events, 0.1 us)
Async XLA Ops:
  7.2 206.0 %all-gather.2.cloned.1.call-start = ((), (), s32[]{:S(2)}) async-start(), calls=%async_computation.2 | async-start | bytes 12976128 | tf_op jit(solution)/shard_map/all_gather | solution.py:13
  7.9 298.0 %reduce-scatter.5.cloned.1.call-start = ((), (), s32[]{:S(2)}) async-start(), calls=%async_computation.4 | async-start | bytes 7077888 | tf_op jit(solution)/shard_map/reduce_scatter | solution.py:37
  8.6 9.3 %copy-start.2 = (s32[1,96]{1,0:T(1,128)S(1)}, s32[1,96]{1,0:T(1,128)}, u32[]{:S(2)}) copy-start(s32[1,96]{1,0:T(1,128)} %param.10) | copy-start | bytes 1156
  225.7 10.7 %copy-start.1 = (s32[1,144]{1,0:T(1,128)S(1)}, s32[1,144]{1,0:T(1,128)}, u32[]{:S(2)}) copy-start(s32[1,144]{1,0:T(1,128)} %param.8) | copy-start | bytes 1732
  225.7 10.8 %copy-start = (bf16[2048,384]{1,0:T(8,128)(2,1)S(1)}, bf16[2048,384]{1,0:T(8,128)(2,1)}, u32[]{:S(2)}) copy-start(bf16[2048,384]{1,0:T(8,128)(2,1)} %param.7) | copy-start | bytes 4718596
  236.1 175.7 %reduce-scatter.3.cloned.1.call-start = ((), (), s32[]{:S(2)}) async-start(), calls=%async_computation.3 | async-start | bytes 10616832 | tf_op jit(solution)/shard_map/reduce_scatter | solution.py:36
Sparse Core Ops, SparseCore 0:
  11.5 201.6 all-gather.1
  236.2 69.5 reduce-scatter.4
  308.4 103.3 reduce-scatter.2
where the time goes:
time: 421 us
  waiting for transfers between devices  329 us (78%)
  local copies, waits for them, and re-layouts  45.5 us (11%)
  matrix products  25.3 us (6%)
  between operations  15.1 us (4%)
  other arithmetic  5.6 us (1%)
    all_gather x1, waiting for transfers between devices, shards(): every_query = lax.all_gather(queries, 'docs', axis=0, tiled=True)  195 us
    reduce_scatter x1, waiting for transfers between devices, shards(): lax.psum_scatter(prefix_terms, 'dims', scatter_dimension=1, tiled=True)  104 us
    reduce_scatter x1, waiting for transfers between devices, shards(): lax.psum_scatter(full_terms, 'dims', scatter_dimension=1, tiled=True)  29.3 us
    gather x2, local copies, waits for them, and re-layouts, pair_products(): picked_queries = jnp.take(query_blocks, pair_ids // local_blocks, axis=0)  26.7 us
    dot_general x2, matrix products, pair_products(): jnp.einsum('gqc,gdc->gqd', picked_queries, picked_docs, preferred_element...  25.3 us
    gather x2, local copies, waits for them, and re-layouts, pair_products(): picked_docs = jnp.take(doc_side, pair_ids % local_blocks, axis=0)  18.8 us
  transfers between devices with their start and end apart: 3, of which 3 were waited for; matrix products, arithmetic and copies ran while one was open for 12% of the time, Pallas kernels for 0%

commit v1 on v0

--- a/solution.py
+++ b/solution.py
@@ -10,7 +10,12 @@
 
 
 def shards(queries, doc_vectors, surv_pairs, surv_count, short_pairs, short_count):
-    every_query = lax.all_gather(queries, "docs", axis=0, tiled=True)
+    every_query = jnp.concatenate(
+        lax.all_to_all(
+            jnp.stack([queries] * lax.axis_size("docs")), "docs", split_axis=0, concat_axis=0
+        ),
+        axis=0,
+    )
     slice_width = queries.shape[1]
     query_blocks = every_query.reshape(-1, QB, slice_width)
     doc_blocks = doc_vectors.reshape(-1, DB, slice_width)

time: 421 us -> 592 us (1.41)
  waiting for transfers between devices: 329 us -> 481 us
  starting transfers between devices: 0.3 us -> 14.7 us
    all_to_all x0 -> x1, waiting for transfers between devices: none -> 306 us  [shards(): lax.all_to_all(jnp.stack([queries] * lax.axis_size('docs')), 'docs', spli...]
    all_gather x1 -> x0, waiting for transfers between devices: 195 us -> none  [shards(): every_query = lax.all_gather(queries, 'docs', axis=0, tiled=True)]
    reduce_scatter x1, waiting for transfers between devices: 29.3 us -> 71.4 us  [shards(): lax.psum_scatter(full_terms, 'dims', scatter_dimension=1, tiled=True)]
    all_to_all x0 -> x1, starting transfers between devices: none -> 14.4 us  [shards(): lax.all_to_all(jnp.stack([queries] * lax.axis_size('docs')), 'docs', spli...]
    another operation x0 -> x1, local copies, waits for them, and re-layouts: none -> 7.42 us  [shards(): jnp.stack([queries] * lax.axis_size('docs'))]
  transfers between devices with their start and end apart: 3 -> 3, of which waited for: 3 -> 3; matrix products, arithmetic and copies ran while one was open for 12% -> 8% of each run, Pallas kernels for 0% -> 0%
where the time goes in v1:
time: 592 us
  waiting for transfers between devices  481 us (81%)
  local copies, waits for them, and re-layouts  51.4 us (9%)
  matrix products  24.7 us (4%)
  between operations  15.4 us (3%)
  starting transfers between devices  14.7 us (2%)
    all_to_all x1, waiting for transfers between devices, shards(): lax.all_to_all(jnp.stack([queries] * lax.axis_size('docs')), 'docs', spli...  306 us
    reduce_scatter x1, waiting for transfers between devices, shards(): lax.psum_scatter(prefix_terms, 'dims', scatter_dimension=1, tiled=True)  104 us
    reduce_scatter x1, waiting for transfers between devices, shards(): lax.psum_scatter(full_terms, 'dims', scatter_dimension=1, tiled=True)  71.4 us
    gather x2, local copies, waits for them, and re-layouts, pair_products(): picked_queries = jnp.take(query_blocks, pair_ids // local_blocks, axis=0)  26.6 us
    dot_general x2, matrix products, pair_products(): jnp.einsum('gqc,gdc->gqd', picked_queries, picked_docs, preferred_element...  24.7 us
    gather x2, local copies, waits for them, and re-layouts, pair_products(): picked_docs = jnp.take(doc_side, pair_ids % local_blocks, axis=0)  17.3 us
    all_to_all x1, starting transfers between devices, shards(): lax.all_to_all(jnp.stack([queries] * lax.axis_size('docs')), 'docs', spli...  14.4 us
  transfers between devices with their start and end apart: 3, of which 3 were waited for; matrix products, arithmetic and copies ran while one was open for 8% of the time, Pallas kernels for 0%

profile of v1, /device:TPU:2, one launch (start us, length us, event | category | flops | bytes accessed | tf_op | source)
XLA Modules:
  0.0 591.9 jit_solution(18099168829980075631)
XLA Ops:
  7.2 7.4 %stack.2 = bf16[32,512,384]{2,1,0:T(8,128)(2,1)} broadcast(bf16[512,384]{1,0:T(8,128)(2,1)} %param.6), dimensions={1,2} | broadcast | bytes 12976128 | tf_op jit(solution)/shard_map/stack | solution.py:15
  14.6 0.0 copy-start.2
  14.6 0.0 copy-start
  14.6 14.4 %all-to-all-start = ((bf16[32,512,384]{2,1,0:T(8,128)(2,1)}), bf16[32,512,384]{2,1,0:T(8,128)(2,1)}, u32[]{:S(2)}, u32[]{:S(2)}) async-start(bf16[32,512,384]{2,1,0:T(8,128)(2,1)} %stack.2), calls=%async_computation | async-start | bytes 25165824 | tf_op jit(solution)/shard_map/all_to_all | solution.py:14
  29.0 0.0 reduce-scatter.5.cloned.1.call-start
  29.1 0.0 copy-done.2
  29.1 0.0 copy-done
  29.1 7.8 %gather_fusion.3 = bf16[96,128,384]{2,1,0:T(8,128)(2,1)} fusion(bf16[16,128,384]{2,1,0:T(8,128)(2,1)S(1)} %bitcast.65, s32[1024]{0:T(1024)S(1)} %get-tuple-element.10), kind=kCustom, calls=%fused_computation.3 | custom fusion | bytes 18874752 | tf_op jit(solution)/shard_map/jit(_take)/gather | solution.py:30
  37.0 305.7 %all-to-all-done = bf16[32,512,384]{2,1,0:T(8,128)(2,1)} async-done(((bf16[32,512,384]{2,1,0:T(8,128)(2,1)}), bf16[32,512,384]{2,1,0:T(8,128)(2,1)}, u32[]{:S(2)}, u32[]{:S(2)}) %all-to-all-start) | async-done | bytes 12582944 | tf_op jit(solution)/shard_map/all_to_all | solution.py:14
  342.6 12.5 %gather_fusion.2 = bf16[96,128,384]{2,1,0:T(8,128)(2,1)} fusion(bf16[128,128,384]{2,1,0:T(8,128)(2,1)} %bitcast.2, s32[1024]{0:T(1024)S(1)} %get-tuple-element.11), kind=kCustom, calls=%fused_computation.2 | custom fusion | bytes 18874752 | tf_op jit(solution)/shard_map/jit(_take)/gather | solution.py:29
  355.1 0.0 copy-start.1
  355.1 10.3 %fusion.5 = f32[96,128,128]{2,1,0:T(8,128)} fusion(bf16[96,128,384]{2,1,0:T(8,128)(2,1)} %gather_fusion.3, bf16[96,128,384]{2,1,0:T(8,128)(2,1)} %gather_fusion.2, pred[96]{0:T(512)(128)(4,1)S(1)} %get-tuple-element.7, pred[96]{0:T(512)(128)(4,1)S(1)} %get-tuple-element.6), kind=kOutput, calls=%fused_computation.9 | convolution fusion | flops 1217396736 | bytes 25166016 | tf_op jit(solution)/shard_map/gqc,gdc->gqd/dot_general | solution.py:31
  365.4 0.0 reduce-scatter.5.cloned.1.call-update
  365.4 0.2 reduce-scatter.3.cloned.1.call-start
  365.7 0.0 copy-done.1
  365.8 0.2 broadcast_select_fusion
  365.9 9.5 %gather_fusion.1 = bf16[144,128,384]{2,1,0:T(8,128)(2,1)} fusion(bf16[16,128,384]{2,1,0:T(8,128)(2,1)S(1)} %broadcast_select_fusion, s32[1024]{0:T(1024)S(1)} %pad_clamp_fusion.2), kind=kCustom, calls=%fused_computation.1 | custom fusion | bytes 28312128 | tf_op jit(solution)/shard_map/jit(_take)/gather | solution.py:30
  375.4 14.1 %gather_fusion = bf16[144,128,384]{2,1,0:T(8,128)(2,1)} fusion(bf16[128,128,384]{2,1,0:T(8,128)(2,1)} %bitcast.2, s32[1024]{0:T(1024)S(1)} %pad_clamp_fusion.3), kind=kCustom, calls=%fused_computation | custom fusion | bytes 28312128 | tf_op jit(solution)/shard_map/jit(_take)/gather | solution.py:29
  389.6 14.3 %fusion = f32[144,128,128]{2,1,0:T(8,128)} fusion(bf16[144,128,384]{2,1,0:T(8,128)(2,1)} %gather_fusion.1, bf16[144,128,384]{2,1,0:T(8,128)(2,1)} %gather_fusion, pred[144]{0:T(512)(128)(4,1)S(1)} %get-tuple-element.5, pred[144]{0:T(512)(128)(4,1)S(1)} %get-tuple-element.4), kind=kOutput, calls=%fused_computation.4 | convolution fusion | flops 1826095104 | bytes 37749024 | tf_op jit(solution)/shard_map/gqc,gdc->gqd/dot_general | solution.py:31
  403.9 0.0 reduce-scatter.3.cloned.1.call-update
  405.3 71.4 %reduce-scatter.5.cloned.1.call-done = f32[96,16,128]{2,1,0:T(8,128)} async-done(((f32[96,128,128]{2,1,0:T(8,128)}), f32[96,16,128]{2,1,0:T(8,128)}) %reduce-scatter.5.cloned.1.call-update) | async-done | bytes 786448 | tf_op jit(solution)/shard_map/reduce_scatter | solution.py:42
  476.7 2.2 select_bitcast_fusion.1
  478.9 103.7 %reduce-scatter.3.cloned.1.call-done = f32[144,16,128]{2,1,0:T(8,128)} async-done(((f32[144,128,128]{2,1,0:T(8,128)}), f32[144,16,128]{2,1,0:T(8,128)}) %reduce-scatter.3.cloned.1.call-update) | async-done | bytes 1179664 | tf_op jit(solution)/shard_map/reduce_scatter | solution.py:41
  582.6 2.5 select_bitcast_fusion
  (11 shorter events, 0.1 us)
Async XLA Ops:
  14.6 14.5 %copy-start.2 = (s32[1,96]{1,0:T(1,128)S(1)}, s32[1,96]{1,0:T(1,128)}, u32[]{:S(2)}) copy-start(s32[1,96]{1,0:T(1,128)} %param.10) | copy-start | bytes 1156
  14.6 14.5 %copy-start = (bf16[2048,384]{1,0:T(8,128)(2,1)S(1)}, bf16[2048,384]{1,0:T(8,128)(2,1)}, u32[]{:S(2)}) copy-start(bf16[2048,384]{1,0:T(8,128)(2,1)} %param.7) | copy-start | bytes 4718596
  14.6 328.0 %all-to-all-start = ((bf16[32,512,384]{2,1,0:T(8,128)(2,1)}), bf16[32,512,384]{2,1,0:T(8,128)(2,1)}, u32[]{:S(2)}, u32[]{:S(2)}) async-start(bf16[32,512,384]{2,1,0:T(8,128)(2,1)} %stack.2), calls=%async_computation | async-start | bytes 25165824 | tf_op jit(solution)/shard_map/all_to_all | solution.py:14
  29.0 447.7 %reduce-scatter.5.cloned.1.call-start = ((), (), s32[]{:S(2)}) async-start(), calls=%async_computation.4 | async-start | bytes 7077888 | tf_op jit(solution)/shard_map/reduce_scatter | solution.py:42
  355.1 10.6 %copy-start.1 = (s32[1,144]{1,0:T(1,128)S(1)}, s32[1,144]{1,0:T(1,128)}, u32[]{:S(2)}) copy-start(s32[1,144]{1,0:T(1,128)} %param.8) | copy-start | bytes 1732
  365.4 217.1 %reduce-scatter.3.cloned.1.call-start = ((), (), s32[]{:S(2)}) async-start(), calls=%async_computation.3 | async-start | bytes 10616832 | tf_op jit(solution)/shard_map/reduce_scatter | solution.py:41
Sparse Core Ops, SparseCore 0:
  365.6 111.0 reduce-scatter.4
  479.2 103.2 reduce-scatter.2
